TPU v7x, 512 devices: a whole 4x4x16 slice. The times are simulated.
512 devices in a mesh: col: 4 (over x_lo, core), gx: 16 (over z), gy: 8 (over x_hi, y).
Axes of the slice: x: 4 (x_hi: 2, x_lo: 2; x = x_hi * 2 + x_lo), y: 4, z: 16, core: 2. Of those that a mesh axis runs over, the one named last changes fastest.
Arguments:
- volume: float32 [32, 8, 64, 1024], P('col', None, 'gx', 'gy'), may hold values from -6 to 6
- filters: float32 [32, 32, 3, 3, 3], P('col'), may hold values from -0.21875 to 0.21875
- upstream: float32 [32, 8, 64, 1024], P('col', None, 'gx', 'gy'), may hold values from -6 to 6
Outputs:
- response: float32 [32, 8, 64, 1024], P('col', None, 'gx', 'gy')
- input_grad: float32 [32, 8, 64, 1024], P('col', None, 'gx', 'gy')
- filter_grad: float32 [32, 32, 3, 3, 3], P('col')
All inputs are finite; a program needn't handle non-finite values.
Results may differ from a plain program's by a relative error of at most 0.0003.
Values sent between devices are 32-bit elements; how exact they have to be, the bound alone decides.
No kernel may reach another device: no remote copies, remote signals or barrier semaphores. Data moves between devices by JAX's collectives and lax.ppermute only.
A program may use at most 64 MiB of HBM per device.

v0:
```python
import jax
import jax.numpy as jnp
from jax import lax
from jax.sharding import PartitionSpec as P


def with_halo(block, sides, width):
    for axis, dim in sides:
        count = lax.axis_size(axis)
        forward = [(i, i + 1) for i in range(count - 1)]
        backward = [(target, source) for source, target in forward]
        low = lax.ppermute(
            lax.slice_in_dim(block, block.shape[dim] - width, None, axis=dim), axis, forward
        )
        high = lax.ppermute(lax.slice_in_dim(block, 0, width, axis=dim), axis, backward)
        block = jnp.concatenate([low, block, high], axis=dim)
    return block


def pad_depth(field):
    return jnp.pad(field, ((0, 0), (1, 1), (0, 0), (0, 0)))


def forward_conv(padded, weights, planes, rows_x, rows_y):
    output = jnp.zeros((weights.shape[0], planes, rows_x, rows_y), jnp.float32)
    for depth in range(3):
        for across in range(3):
            for along in range(3):
                window = padded[
                    :, depth : depth + planes, across : across + rows_x, along : along + rows_y
                ]
                output = output + jnp.einsum(
                    "oc,czxy->ozxy",
                    weights[:, :, depth, across, along],
                    window,
                    precision=lax.Precision.HIGHEST,
                )
    return output


def backward_conv(padded_up, weights, planes, rows_x, rows_y):
    output = jnp.zeros((weights.shape[1], planes, rows_x, rows_y), jnp.float32)
    for depth in range(3):
        for across in range(3):
            for along in range(3):
                window = padded_up[
                    :,
                    2 - depth : 2 - depth + planes,
                    2 - across : 2 - across + rows_x,
                    2 - along : 2 - along + rows_y,
                ]
                output = output + jnp.einsum(
                    "oc,ozxy->czxy",
                    weights[:, :, depth, across, along],
                    window,
                    precision=lax.Precision.HIGHEST,
                )
    return output


def weight_terms(cotangent, padded, planes, rows_x, rows_y):
    pieces = []
    for depth in range(3):
        for across in range(3):
            for along in range(3):
                window = padded[
                    :, depth : depth + planes, across : across + rows_x, along : along + rows_y
                ]
                pieces.append(
                    jnp.einsum("ozxy,czxy->oc", cotangent, window, precision=lax.Precision.HIGHEST)
                )
    stacked = jnp.stack(pieces, axis=-1)
    return stacked.reshape(stacked.shape[0], stacked.shape[1], 3, 3, 3)


def shards(volume, filters, upstream):
    planes, rows_x, rows_y = (volume.shape[1], volume.shape[2], volume.shape[3])
    own_inputs = volume.shape[0]
    scale = (planes * rows_x * lax.axis_size("gx") * rows_y * lax.axis_size("gy")) ** (-0.5)
    gathered = lax.all_gather(volume, "col", axis=0, tiled=True)
    padded = pad_depth(with_halo(gathered, (("gx", 2), ("gy", 3)), 1))
    response = forward_conv(padded, filters, planes, rows_x, rows_y)
    all_rows = lax.all_gather(filters, "col", axis=0, tiled=True)
    all_upstream = lax.all_gather(upstream, "col", axis=0, tiled=True)
    padded_up = pad_depth(with_halo(all_upstream, (("gx", 2), ("gy", 3)), 1))
    first = lax.axis_index("col") * own_inputs
    own_filters = lax.dynamic_slice_in_dim(all_rows, first, own_inputs, 1)
    input_grad = backward_conv(padded_up, own_filters, planes, rows_x, rows_y)
    local_grad = weight_terms(upstream, padded, planes, rows_x, rows_y)
    ncol = lax.axis_size("col")
    flat = local_grad.reshape(-1, 128)
    slots = jnp.zeros((ncol,) + flat.shape, jnp.float32)
    slots = lax.dynamic_update_index_in_dim(slots, flat, lax.axis_index("col"), 0)
    summed = lax.psum(slots, ("col", "gx", "gy"))
    total_grad = summed[lax.axis_index("col")].reshape(local_grad.shape)
    return (response, input_grad, total_grad * scale)


def solution(mesh):
    placed = (
        P("col", None, "gx", "gy"),
        P("col", None, None, None, None),
        P("col", None, "gx", "gy"),
    )
    return jax.shard_map(
        shards,
        mesh=mesh,
        in_specs=placed,
        out_specs=(
            P("col", None, "gx", "gy"),
            P("col", None, "gx", "gy"),
            P("col", None, None, None, None),
        ),
        check_vma=False,
    )
```

profile of v0, /device:TPU:1, one launch (start us, length us, event | category | flops | bytes accessed | tf_op | source)
XLA Modules:
  0.0 655.5 jit_solution(1451040845485001192)
XLA Ops:
  8.2 13.2 %all_gather.9 = f32[32,8,4,128]{3,0,2,1:T(8,128)S(1)} all-gather(f32[8,8,4,128]{3,0,2,1:T(8,128)S(1)} %copy.126), channel_id=1, replica_groups=mesh['col'=4,'gx'=16,'gy'=8] {'col'}, dimensions={0}, use_global_device_ids=true | all-gather | bytes 655360 | tf_op jit(solution)/shard_map/all_gather | solution.py:80
  25.7 7.3 %all_gather.11 = f32[32,8,4,128]{3,0,2,1:T(8,128)S(1)} all-gather(f32[8,8,4,128]{3,0,2,1:T(8,128)S(1)} %copy.134), channel_id=1, replica_groups=mesh['col'=4,'gx'=16,'gy'=8] {'col'}, dimensions={0}, use_global_device_ids=true | all-gather | bytes 655360 | tf_op jit(solution)/shard_map/all_gather | solution.py:84
  33.7 4.6 collective-permute-start.4
  39.6 6.8 %all_gather.10 = f32[32,32,3,3,3]{1,0,4,3,2:T(8,128)S(1)} all-gather(f32[8,32,3,3,3]{1,0,4,3,2:T(8,128)S(1)} %copy-done.66), channel_id=1, replica_groups=mesh['col'=4,'gx'=16,'gy'=8] {'col'}, dimensions={0}, use_global_device_ids=true | all-gather | bytes 138240 | tf_op jit(solution)/shard_map/all_gather | solution.py:83
  49.9 1.9 collective-permute-start.2
  57.2 2.1 copy.135
  59.2 4.6 collective-permute-start.6
  68.3 2.0 fusion.116
  70.4 2.0 fusion.112
  75.6 2.9 pad_maximum_fusion.9
  78.5 2.1 select_maximum_fusion.2
  81.7 2.0 copy.138
  83.7 1.9 select_maximum_fusion
  111.9 4.3 fusion.309
  116.2 1.8 fusion.212
  121.6 1.8 fusion.218
  123.4 1.8 fusion.220
  127.0 1.9 fusion.224
  128.9 1.9 fusion.226
  132.6 1.9 convolution_bitcast_fusion.7
  134.5 1.9 convolution_bitcast_fusion.8
  182.0 2.0 fusion.47
  193.8 2.1 fusion.48
  199.9 445.2 %all-reduce.4.cloned.1.call-done = f32[4,54,128]{2,1,0:T(8,128)} async-done(((f32[4,54,128]{2,1,0:T(8,128)}), f32[4,54,128]{2,1,0:T(8,128)}) %all-reduce.4.cloned.1.call-update) | async-done | bytes 110608 | tf_op jit(solution)/shard_map/psum | solution.py:94
  (246 shorter events, 120.0 us)
Async XLA Ops:
  7.2 32.4 %copy-start.66 = (f32[8,32,3,3,3]{1,0,4,3,2:T(8,128)S(1)}, f32[8,32,3,3,3]{1,0,4,3,2:T(8,128)}, u32[]{:S(2)}) copy-start(f32[8,32,3,3,3]{1,0,4,3,2:T(8,128)} %param.4) | copy-start | bytes 82948
  7.2 637.9 %all-reduce.4.cloned.1.call-start = ((), (), s32[]{:S(2)}) async-start(), calls=%async_computation | async-start | bytes 229376 | tf_op jit(solution)/shard_map/psum | solution.py:94
  21.4 26.4 %copy-start.3 = (f32[32,8,4,128]{3,0,2,1:T(8,128)}, f32[32,8,4,128]{3,0,2,1:T(8,128)S(1)}, u32[]{:S(2)}) copy-start(f32[32,8,4,128]{3,0,2,1:T(8,128)S(1)} %all_gather.9) | copy-start | bytes 1572868
  22.1 25.5 %collective-permute-start = (f32[32,8,1,128]{3,0,2,1:T(8,128)S(1)}, f32[32,8,1,128]{3,0,2,1:T(8,128)S(1)}, u32[]{:S(2)}, u32[]{:S(2)}) collective-permute-start(f32[32,8,1,128]{3,0,2,1:T(8,128)S(1)} %get-tuple-element.49), channel_id=1, source_target_pairs={{0,8},{8,16},{16,24},{24,32},{32,40},{40,48},{48,56},{56,64},{64,7... | collective-permute-start | bytes 393224 | tf_op jit(solution)/shard_map/ppermute | solution.py:12
  23.4 24.4 %collective-permute-start.1 = (f32[32,8,1,128]{3,0,2,1:T(8,128)}, f32[32,8,1,128]{3,0,2,1:T(8,128)S(1)}, u32[]{:S(2)}, u32[]{:S(2)}) collective-permute-start(f32[32,8,1,128]{3,0,2,1:T(8,128)} %get-tuple-element.48), channel_id=1, source_target_pairs={{8,0},{16,8},{24,16},{32,24},{40,32},{48,40},{56,48},{64,56},{72,6... | collective-permute-start | bytes 393224 | tf_op jit(solution)/shard_map/ppermute | solution.py:15
  33.7 20.4 %collective-permute-start.4 = (f32[32,8,1,128]{3,0,2,1:T(8,128)}, f32[32,8,1,128]{3,0,2,1:T(8,128)}, u32[]{:S(2)}, u32[]{:S(2)}) collective-permute-start(f32[32,8,1,128]{3,0,2,1:T(8,128)} %get-tuple-element.44), channel_id=1, source_target_pairs={{0,8},{8,16},{16,24},{24,32},{32,40},{40,48},{48,56},{56,64},{64,7... | collective-permute-start | bytes 393224 | tf_op jit(solution)/shard_map/ppermute | solution.py:12
  38.3 16.7 %collective-permute-start.5 = (f32[32,8,1,128]{3,0,2,1:T(8,128)}, f32[32,8,1,128]{3,0,2,1:T(8,128)}, u32[]{:S(2)}, u32[]{:S(2)}) collective-permute-start(f32[32,8,1,128]{3,0,2,1:T(8,128)} %get-tuple-element.43), channel_id=1, source_target_pairs={{8,0},{16,8},{24,16},{32,24},{40,32},{48,40},{56,48},{64,56},{72,6... | collective-permute-start | bytes 393224 | tf_op jit(solution)/shard_map/ppermute | solution.py:15
  49.9 22.5 %collective-permute-start.2 = (f32[32,8,6,1]{0,1,3,2:T(8,128)}, f32[32,8,6,1]{0,1,3,2:T(8,128)}, u32[]{:S(2)}, u32[]{:S(2)}) collective-permute-start(f32[32,8,6,1]{0,1,3,2:T(8,128)} %copy.127), channel_id=1, source_target_pairs={{0,1},{1,2},{2,3},{3,4},{4,5},{5,6},{6,7},{8,9},{9,10},{10,11},{11... | collective-permute-start | bytes 18440 | tf_op jit(solution)/shard_map/ppermute | solution.py:12
  52.8 20.7 %collective-permute-start.3 = (f32[32,8,6,1]{0,1,3,2:T(8,128)}, f32[32,8,6,1]{0,1,3,2:T(8,128)}, u32[]{:S(2)}, u32[]{:S(2)}) collective-permute-start(f32[32,8,6,1]{0,1,3,2:T(8,128)} %copy.128), channel_id=1, source_target_pairs={{1,0},{2,1},{3,2},{4,3},{5,4},{6,5},{7,6},{9,8},{10,9},{11,10},{12... | collective-permute-start | bytes 18440 | tf_op jit(solution)/shard_map/ppermute | solution.py:15
  56.0 10.6 %copy-start.20 = (f32[32,8,5,128]{3,0,2,1:T(8,128)S(1)}, f32[32,8,5,128]{3,0,2,1:T(8,128)}, u32[]{:S(2)}) copy-start(f32[32,8,5,128]{3,0,2,1:T(8,128)} %copy-done.19) | copy-start | bytes 1966084
  59.2 21.3 %collective-permute-start.6 = (f32[32,8,6,1]{0,1,3,2:T(8,128)}, f32[32,8,6,1]{0,1,3,2:T(8,128)}, u32[]{:S(2)}, u32[]{:S(2)}) collective-permute-start(f32[32,8,6,1]{0,1,3,2:T(8,128)} %copy.135), channel_id=1, source_target_pairs={{0,1},{1,2},{2,3},{3,4},{4,5},{5,6},{6,7},{8,9},{9,10},{10,11},{11... | collective-permute-start | bytes 18440 | tf_op jit(solution)/shard_map/ppermute | solution.py:12
  64.8 16.9 %collective-permute-start.7 = (f32[32,8,6,1]{0,1,3,2:T(8,128)}, f32[32,8,6,1]{0,1,3,2:T(8,128)}, u32[]{:S(2)}, u32[]{:S(2)}) collective-permute-start(f32[32,8,6,1]{0,1,3,2:T(8,128)} %copy.136), channel_id=1, source_target_pairs={{1,0},{2,1},{3,2},{4,3},{5,4},{6,5},{7,6},{9,8},{10,9},{11,10},{12... | collective-permute-start | bytes 18440 | tf_op jit(solution)/shard_map/ppermute | solution.py:15
  85.5 22.5 %copy-start.1 = (f32[32,10,6,130]{3,0,2,1:T(8,128)}, f32[32,10,6,130]{3,0,2,1:T(8,128)S(1)}, u32[]{:S(2)}) copy-start(f32[32,10,6,130]{3,0,2,1:T(8,128)S(1)} %select_maximum_fusion) | copy-start | bytes 2995204
  127.0 11.2 %copy-start = (f32[8,8,4,128]{3,2,1,0:T(4,128)S(1)}, f32[8,8,4,128]{3,2,1,0:T(4,128)}, u32[]{:S(2)}) copy-start(f32[8,8,4,128]{3,2,1,0:T(4,128)} %param.5) | copy-start | bytes 393220
  127.0 11.2 %copy-start.33 = (f32[32,8,4,128]{3,0,2,1:T(8,128)S(1)}, f32[32,8,4,128]{3,0,2,1:T(8,128)}, u32[]{:S(2)}) copy-start(f32[32,8,4,128]{3,0,2,1:T(8,128)} %get-tuple-element.29) | copy-start | bytes 1572868
  128.9 10.4 %copy-start.13 = (f32[32,8,4,128]{3,0,2,1:T(8,128)S(1)}, f32[32,8,4,128]{3,0,2,1:T(8,128)}, u32[]{:S(2)}) copy-start(f32[32,8,4,128]{3,0,2,1:T(8,128)} %get-tuple-element.31) | copy-start | bytes 1572868
  130.8 10.3 %copy-start.32 = (f32[32,8,4,128]{3,0,2,1:T(8,128)S(1)}, f32[32,8,4,128]{3,0,2,1:T(8,128)}, u32[]{:S(2)}) copy-start(f32[32,8,4,128]{3,0,2,1:T(8,128)} %get-tuple-element.28) | copy-start | bytes 1572868
  132.6 9.7 %copy-start.31 = (f32[32,8,4,128]{3,0,2,1:T(8,128)S(1)}, f32[32,8,4,128]{3,0,2,1:T(8,128)}, u32[]{:S(2)}) copy-start(f32[32,8,4,128]{3,0,2,1:T(8,128)} %get-tuple-element.27) | copy-start | bytes 1572868
  134.5 8.9 %copy-start.30 = (f32[32,8,4,128]{3,0,2,1:T(8,128)S(1)}, f32[32,8,4,128]{3,0,2,1:T(8,128)}, u32[]{:S(2)}) copy-start(f32[32,8,4,128]{3,0,2,1:T(8,128)} %get-tuple-element.26) | copy-start | bytes 1572868
  150.2 8.4 %copy-start.4 = (f32[32,8,4,128]{3,0,2,1:T(8,128)S(1)}, f32[32,8,4,128]{3,0,2,1:T(8,128)}, u32[]{:S(2)}) copy-start(f32[32,8,4,128]{3,0,2,1:T(8,128)} %copy-done.3) | copy-start | bytes 1572868
  151.6 8.2 %copy-start.10 = (f32[32,8,4,128]{3,0,2,1:T(8,128)S(1)}, f32[32,8,4,128]{3,0,2,1:T(8,128)}, u32[]{:S(2)}) copy-start(f32[32,8,4,128]{3,0,2,1:T(8,128)} %get-tuple-element.38) | copy-start | bytes 1572868
  152.7 8.8 %copy-start.14 = (f32[32,8,4,128]{3,0,2,1:T(8,128)S(1)}, f32[32,8,4,128]{3,0,2,1:T(8,128)}, u32[]{:S(2)}) copy-start(f32[32,8,4,128]{3,0,2,1:T(8,128)} %get-tuple-element.40) | copy-start | bytes 1572868
  154.5 8.2 %copy-start.8 = (f32[32,8,4,128]{3,0,2,1:T(8,128)S(1)}, f32[32,8,4,128]{3,0,2,1:T(8,128)}, u32[]{:S(2)}) copy-start(f32[32,8,4,128]{3,0,2,1:T(8,128)} %get-tuple-element.30) | copy-start | bytes 1572868
  155.7 8.2 %copy-start.17 = (f32[32,8,5,128]{3,0,2,1:T(8,128)S(1)}, f32[32,8,5,128]{3,0,2,1:T(8,128)}, u32[]{:S(2)}) copy-start(f32[32,8,5,128]{3,0,2,1:T(8,128)} %copy-done.16) | copy-start | bytes 1966084
  (52 other events, 259.5 us)
Sparse Core Ops, SparseCore 0:
  182.0 463.0 all-reduce.3
where the time goes:
time: 660 us; the launch traced here: 655 us
  waiting for transfers between devices  445 us (67%)
  matrix products  109 us (17%)
  local copies, waits for them, and re-layouts  32.7 us (5%)
  blocking collectives  27.3 us (4%)
  starting transfers between devices  18.1 us (3%)
  between operations  15.4 us (2%)
  other arithmetic  7.59 us (1%)
    psum x1, waiting for transfers between devices, shards(): summed = lax.psum(slots, ('col', 'gx', 'gy'))  445 us
    dot_general x27, matrix products, forward_conv(): jnp.einsum('oc,czxy->ozxy', weights[:, :, depth, across, along], window,...  43.3 us
    dot_general x27, matrix products, backward_conv(): jnp.einsum('oc,ozxy->czxy', weights[:, :, depth, across, along], window,...  35 us
    dot_general x27, matrix products, weight_terms(): jnp.einsum('ozxy,czxy->oc', cotangent, window, precision=lax.Precision.HI...  30.8 us
  transfers between devices with their start and end apart: 9, of which 1 were waited for; matrix products, arithmetic and copies ran while one was open for 7% of the time, Pallas kernels for 0%

commit v1 on v0

--- a/solution.py
+++ b/solution.py
@@ -77,7 +77,9 @@
     planes, rows_x, rows_y = (volume.shape[1], volume.shape[2], volume.shape[3])
     own_inputs = volume.shape[0]
     scale = (planes * rows_x * lax.axis_size("gx") * rows_y * lax.axis_size("gy")) ** (-0.5)
-    gathered = lax.all_gather(volume, "col", axis=0, tiled=True)
+    gathered = jnp.concatenate(
+        lax.all_to_all(jnp.stack([volume] * lax.axis_size("col")), "col", 0, 0), axis=0
+    )
     padded = pad_depth(with_halo(gathered, (("gx", 2), ("gy", 3)), 1))
     response = forward_conv(padded, filters, planes, rows_x, rows_y)
     all_rows = lax.all_gather(filters, "col", axis=0, tiled=True)

time: 660 us -> 637 us (0.965)
  matrix products: 109 us -> 82.1 us
  waiting for transfers between devices: 445 us -> 461 us
  starting transfers between devices: 18.1 us -> 27.2 us
  local copies, waits for them, and re-layouts: 32.7 us -> 23.9 us
  blocking collectives: 27.3 us -> 19.1 us
    dot_general x27, matrix products: 35 us -> 16.8 us  [backward_conv(): jnp.einsum('oc,ozxy->czxy', weights[:, :, depth, across, along], window,...]
    all_gather x1 -> x0, blocking collectives: 13.2 us -> none  [shards(): gathered = lax.all_gather(volume, 'col', axis=0, tiled=True)]
    psum x1, waiting for transfers between devices: 445 us -> 458 us  [shards(): summed = lax.psum(slots, ('col', 'gx', 'gy'))]
    all_to_all x0 -> x1, starting transfers between devices: none -> 10.3 us  [shards(): lax.all_to_all(jnp.stack([volume] * lax.axis_size('col')), 'col', 0, 0)]
    dot_general x27, matrix products: 43.3 us -> 34.2 us  [forward_conv(): jnp.einsum('oc,czxy->ozxy', weights[:, :, depth, across, along], window,...]
  transfers between devices with their start and end apart: 9 -> 10, of which waited for: 1 -> 2; matrix products, arithmetic and copies ran while one was open for 7% -> 5% of each run, Pallas kernels for 0% -> 0%
where the time goes in v1:
time: 637 us; the launch traced here: 634 us
  waiting for transfers between devices  461 us (72%)
  matrix products  82.1 us (13%)
  starting transfers between devices  27.2 us (4%)
  local copies, waits for them, and re-layouts  23.9 us (4%)
  blocking collectives  19.1 us (3%)
  between operations  15.1 us (2%)
    psum x1, waiting for transfers between devices, shards(): summed = lax.psum(slots, ('col', 'gx', 'gy'))  458 us
    dot_general x27, matrix products, forward_conv(): jnp.einsum('oc,czxy->ozxy', weights[:, :, depth, across, along], window,...  34.2 us
    dot_general x27, matrix products, weight_terms(): jnp.einsum('ozxy,czxy->oc', cotangent, window, precision=lax.Precision.HI...  31.1 us
    dot_general x27, matrix products, backward_conv(): jnp.einsum('oc,ozxy->czxy', weights[:, :, depth, across, along], window,...  16.8 us
  transfers between devices with their start and end apart: 10, of which 2 were waited for; matrix products, arithmetic and copies ran while one was open for 5% of the time, Pallas kernels for 0%

profile of v1, /device:TPU:1, one launch (start us, length us, event | category | flops | bytes accessed | tf_op | source)
XLA Modules:
  0.0 633.7 jit_solution(12122410551650406626)
XLA Ops:
  9.1 10.3 %all-to-all-start = ((f32[4,8,8,4,128]{4,1,3,2,0:T(8,128)}), f32[4,8,8,4,128]{4,1,3,2,0:T(8,128)S(1)}, u32[]{:S(2)}, u32[]{:S(2)}) async-start(f32[4,8,8,4,128]{4,1,3,2,0:T(8,128)} %stack.91), calls=%async_computation | async-start | bytes 1048576 | tf_op jit(solution)/shard_map/all_to_all | solution.py:81
  19.4 12.2 %all_gather.7 = f32[32,8,4,128]{3,0,2,1:T(8,128)S(1)} all-gather(f32[8,8,4,128]{3,0,2,1:T(8,128)S(1)} %copy.135), channel_id=1, replica_groups=mesh['col'=4,'gx'=16,'gy'=8] {'col'}, dimensions={0}, use_global_device_ids=true | all-gather | bytes 655360 | tf_op jit(solution)/shard_map/all_gather | solution.py:86
  34.3 6.8 %all_gather.6 = f32[32,32,3,3,3]{1,0,4,3,2:T(8,128)S(1)} all-gather(f32[8,32,3,3,3]{1,0,4,3,2:T(8,128)S(1)} %copy-done.42), channel_id=1, replica_groups=mesh['col'=4,'gx'=16,'gy'=8] {'col'}, dimensions={0}, use_global_device_ids=true | all-gather | bytes 138240 | tf_op jit(solution)/shard_map/all_gather | solution.py:85
  46.5 1.8 collective-permute-start.7
  48.3 1.4 fusion.120
  49.7 1.4 fusion.116
  66.7 4.0 collective-permute-start
  73.1 3.3 collective-permute-done.1
  77.2 4.5 collective-permute-start.2
  82.0 1.5 collective-permute-start.3
  83.5 1.7 fusion.78
  85.3 1.7 convolution_bitcast_fusion
  90.6 2.1 select_maximum_fusion.2
  92.7 4.4 fusion.321
  97.1 1.9 fusion.216
  99.0 1.8 fusion.218
  100.8 1.8 fusion.220
  154.2 1.7 copy.196
  155.9 1.7 broadcast_in_dim.8
  159.8 1.9 fusion.48
  161.6 1.7 fusion.11
  163.5 1.5 fusion.40
  165.7 457.6 %all-reduce.4.cloned.1.call-done = f32[4,54,128]{2,1,0:T(8,128)} async-done(((f32[4,54,128]{2,1,0:T(8,128)}), f32[4,54,128]{2,1,0:T(8,128)}) %all-reduce.4.cloned.1.call-update) | async-done | bytes 110608 | tf_op jit(solution)/shard_map/psum | solution.py:96
  624.9 1.6 copy.199
  (203 shorter events, 88.1 us)
Async XLA Ops:
  7.2 12.2 %copy-start = (f32[8,8,4,128]{3,2,1,0:T(4,128)S(1)}, f32[8,8,4,128]{3,2,1,0:T(4,128)}, u32[]{:S(2)}) copy-start(f32[8,8,4,128]{3,2,1,0:T(4,128)} %param.5) | copy-start | bytes 393220
  7.2 27.1 %copy-start.42 = (f32[8,32,3,3,3]{1,0,4,3,2:T(8,128)S(1)}, f32[8,32,3,3,3]{1,0,4,3,2:T(8,128)}, u32[]{:S(2)}) copy-start(f32[8,32,3,3,3]{1,0,4,3,2:T(8,128)} %param.4) | copy-start | bytes 82948
  9.1 57.6 %all-to-all-start = ((f32[4,8,8,4,128]{4,1,3,2,0:T(8,128)}), f32[4,8,8,4,128]{4,1,3,2,0:T(8,128)S(1)}, u32[]{:S(2)}, u32[]{:S(2)}) async-start(f32[4,8,8,4,128]{4,1,3,2,0:T(8,128)} %stack.91), calls=%async_computation | async-start | bytes 1048576 | tf_op jit(solution)/shard_map/all_to_all | solution.py:81
  19.4 604.0 %all-reduce.4.cloned.1.call-start = ((), (), s32[]{:S(2)}) async-start(), calls=%async_computation.1 | async-start | bytes 229376 | tf_op jit(solution)/shard_map/psum | solution.py:96
  31.7 10.6 %collective-permute-start.4 = (f32[32,8,1,128]{3,0,2,1:T(8,128)S(1)}, f32[32,8,1,128]{3,0,2,1:T(8,128)S(1)}, u32[]{:S(2)}, u32[]{:S(2)}) collective-permute-start(f32[32,8,1,128]{3,0,2,1:T(8,128)S(1)} %get-tuple-element.45), channel_id=1, source_target_pairs={{0,8},{8,16},{16,24},{24,32},{32,40},{40,48},{48,56},{56,64},{64,7... | collective-permute-start | bytes 393224 | tf_op jit(solution)/shard_map/ppermute | solution.py:12
  33.0 9.3 %collective-permute-start.5 = (f32[32,8,1,128]{3,0,2,1:T(8,128)S(1)}, f32[32,8,1,128]{3,0,2,1:T(8,128)S(1)}, u32[]{:S(2)}, u32[]{:S(2)}) collective-permute-start(f32[32,8,1,128]{3,0,2,1:T(8,128)S(1)} %get-tuple-element.44), channel_id=1, source_target_pairs={{8,0},{16,8},{24,16},{32,24},{40,32},{48,40},{56,48},{64,56},{72,6... | collective-permute-start | bytes 393224 | tf_op jit(solution)/shard_map/ppermute | solution.py:15
  44.9 6.2 collective-permute-start.6
  46.5 5.0 collective-permute-start.7
  66.7 6.4 %collective-permute-start = (f32[32,8,1,128]{3,0,2,1:T(8,128)S(1)}, f32[32,8,1,128]{3,0,2,1:T(8,128)S(1)}, u32[]{:S(2)}, u32[]{:S(2)}) collective-permute-start(f32[32,8,1,128]{3,0,2,1:T(8,128)S(1)} %get-tuple-element.46), channel_id=1, source_target_pairs={{0,8},{8,16},{16,24},{24,32},{32,40},{40,48},{48,56},{56,64},{64,7... | collective-permute-start | bytes 393224 | tf_op jit(solution)/shard_map/ppermute | solution.py:12
  70.8 5.7 collective-permute-start.1
  77.2 10.9 %collective-permute-start.2 = (f32[32,8,6,1]{0,1,3,2:T(8,128)S(1)}, f32[32,8,6,1]{0,1,3,2:T(8,128)S(1)}, u32[]{:S(2)}, u32[]{:S(2)}) collective-permute-start(f32[32,8,6,1]{0,1,3,2:T(8,128)S(1)} %copy.128), channel_id=1, source_target_pairs={{0,1},{1,2},{2,3},{3,4},{4,5},{5,6},{6,7},{8,9},{9,10},{10,11},{11... | collective-permute-start | bytes 18440 | tf_op jit(solution)/shard_map/ppermute | solution.py:12
  82.0 7.3 %collective-permute-start.3 = (f32[32,8,6,1]{0,1,3,2:T(8,128)S(1)}, f32[32,8,6,1]{0,1,3,2:T(8,128)S(1)}, u32[]{:S(2)}, u32[]{:S(2)}) collective-permute-start(f32[32,8,6,1]{0,1,3,2:T(8,128)S(1)} %copy.129), channel_id=1, source_target_pairs={{1,0},{2,1},{3,2},{4,3},{5,4},{6,5},{7,6},{9,8},{10,9},{11,10},{12... | collective-permute-start | bytes 18440 | tf_op jit(solution)/shard_map/ppermute | solution.py:15
  100.8 7.5 %copy-start.3 = (f32[32,8,6,1]{3,0,2,1:T(8,128)S(1)}, f32[32,8,6,1]{3,0,2,1:T(8,128)}, u32[]{:S(2)}) copy-start(f32[32,8,6,1]{3,0,2,1:T(8,128)} %copy.130) | copy-start | bytes 18436
  100.8 7.5 %copy-start.4 = (f32[32,8,6,1]{3,0,2,1:T(8,128)S(1)}, f32[32,8,6,1]{3,0,2,1:T(8,128)}, u32[]{:S(2)}) copy-start(f32[32,8,6,1]{3,0,2,1:T(8,128)} %copy.131) | copy-start | bytes 18436
  109.0 12.8 %copy-start.2 = (f32[32,8,6,129]{3,0,2,1:T(8,128)}, f32[32,8,6,129]{3,0,2,1:T(8,128)S(1)}, u32[]{:S(2)}) copy-start(f32[32,8,6,129]{3,0,2,1:T(8,128)S(1)} %get-tuple-element.39) | copy-start | bytes 2377732
  148.4 11.2 %copy-start.21 = (f32[8,4,128,8]{2,3,1,0:T(8,128)S(1)}, f32[8,4,128,8]{2,3,1,0:T(8,128)}, u32[]{:S(2)}) copy-start(f32[8,4,128,8]{2,3,1,0:T(8,128)} %fusion.216) | copy-start | bytes 393220
  148.4 11.3 %copy-start.22 = (f32[8,4,128,8]{2,3,1,0:T(8,128)S(1)}, f32[8,4,128,8]{2,3,1,0:T(8,128)}, u32[]{:S(2)}) copy-start(f32[8,4,128,8]{2,3,1,0:T(8,128)} %fusion.218) | copy-start | bytes 393220
  148.4 11.3 %copy-start.23 = (f32[8,4,128,8]{2,3,1,0:T(8,128)S(1)}, f32[8,4,128,8]{2,3,1,0:T(8,128)}, u32[]{:S(2)}) copy-start(f32[8,4,128,8]{2,3,1,0:T(8,128)} %fusion.220) | copy-start | bytes 393220
  148.4 11.3 %copy-start.24 = (f32[8,4,128,8]{2,3,1,0:T(8,128)S(1)}, f32[8,4,128,8]{2,3,1,0:T(8,128)}, u32[]{:S(2)}) copy-start(f32[8,4,128,8]{2,3,1,0:T(8,128)} %fusion.222) | copy-start | bytes 393220
  148.4 11.3 %copy-start.25 = (f32[8,4,128,8]{2,3,1,0:T(8,128)S(1)}, f32[8,4,128,8]{2,3,1,0:T(8,128)}, u32[]{:S(2)}) copy-start(f32[8,4,128,8]{2,3,1,0:T(8,128)} %fusion.224) | copy-start | bytes 393220
  148.4 11.3 %copy-start.26 = (f32[8,4,128,8]{2,3,1,0:T(8,128)S(1)}, f32[8,4,128,8]{2,3,1,0:T(8,128)}, u32[]{:S(2)}) copy-start(f32[8,4,128,8]{2,3,1,0:T(8,128)} %fusion.226) | copy-start | bytes 393220
  148.4 11.3 %copy-start.27 = (f32[8,4,128,8]{2,3,1,0:T(8,128)S(1)}, f32[8,4,128,8]{2,3,1,0:T(8,128)}, u32[]{:S(2)}) copy-start(f32[8,4,128,8]{2,3,1,0:T(8,128)} %fusion.228) | copy-start | bytes 393220
  148.4 11.3 %copy-start.28 = (f32[8,4,128,8]{2,3,1,0:T(8,128)S(1)}, f32[8,4,128,8]{2,3,1,0:T(8,128)}, u32[]{:S(2)}) copy-start(f32[8,4,128,8]{2,3,1,0:T(8,128)} %fusion.230) | copy-start | bytes 393220
  154.2 9.2 %copy-start.29 = (f32[8,8,4,128]{3,0,2,1:T(8,128)S(1)}, f32[8,8,4,128]{3,0,2,1:T(8,128)}, u32[]{:S(2)}) copy-start(f32[8,8,4,128]{3,0,2,1:T(8,128)} %convolution_bitcast_fusion.2) | copy-start | bytes 393220
  (30 other events, 144.8 us)
Sparse Core Ops, SparseCore 0:
  159.7 463.5 all-reduce.3
